TPU v7x, 32 devices: a whole 2x2x4 slice. The times are simulated.
32 devices in a mesh: dp: 16 (over z, y, core), head: 2 (over x).
Axes of the slice: x: 2, y: 2, z: 4, core: 2. Of those that a mesh axis runs over, the one named last changes fastest.
Arguments:
- layer_input: bfloat16 [16, 256, 768], P('dp', 'head'), may hold values from -6 to 6
- pair_input: bfloat16 [16, 256, 256, 256], P('dp', 'head'), may hold values from -6 to 6
- time_cond: float32 [16, 256], P('dp'), may hold values from -6 to 6
- chain_lengths: int32 [16], P('dp'), may hold values from 128 to 256, as said below
- residue_mask: int32 [16, 256], P('dp'), may hold values from 0 to 1, as said below
- mod_weight: bfloat16 [256, 4608], replicated, may hold values from -0.375 to 0.375
- mod_bias: float32 [4608], replicated, may hold values from -3 to 3
- qkv_weight: bfloat16 [768, 3, 768], P(None, None, 'head'), may hold values from -0.21875 to 0.21875
- pair_gain: float32 [256], replicated, may hold values from 0.25 to 1.75
- pair_weight: bfloat16 [256, 12], replicated, may hold values from -0.375 to 0.375
- out_weight: bfloat16 [768, 768], P('head'), may hold values from -0.625 to 0.625
- out_bias: float32 [768], replicated, may hold values from -3 to 3
- gate_up_weight: bfloat16 [768, 2, 3072], P(None, None, 'head'), may hold values from -0.21875 to 0.21875
- down_weight: bfloat16 [3072, 768], P('head'), may hold values from -0.21875 to 0.21875
- output_grad: bfloat16 [16, 256, 768], P('dp', 'head'), may hold values from -6 to 6
Outputs:
- layer_output: bfloat16 [16, 256, 768], P('dp', 'head')
- input_grad: float32 [16, 256, 768], P('dp', 'head')
- pair_grad: bfloat16 [16, 256, 256, 256], P('dp', 'head')
- cond_grad: float32 [16, 256], P('dp')
- mod_weight_grad: float32 [256, 4608], replicated
- mod_bias_grad: float32 [4608], replicated
- qkv_weight_grad: float32 [768, 3, 768], P('dp', None, 'head')
- pair_gain_grad: float32 [256], replicated
- pair_weight_grad: float32 [256, 12], replicated
- out_weight_grad: float32 [768, 768], P('head', 'dp')
- out_bias_grad: float32 [768], replicated
- gate_up_grad: float32 [768, 2, 3072], P('dp', None, 'head')
- down_grad: float32 [3072, 768], P('head', 'dp')
Inputs may be any that keep to these rules, and one draw needn't show every extreme that they name: `chain_lengths`: each chain has 128 to 256 residues in use; the first chain has all 256. `residue_mask`: the first residue of every chain is resolved.
All inputs are finite; a program needn't handle non-finite values.
Results may differ from a plain program's by a relative error of at most 0.014.
The roundings to bfloat16 on the way count: a program that leaves them out, or rounds other values in their place, can miss the bound.
Values may be sent and summed in bfloat16 or wider, within the bound.
No kernel may reach another device: no remote copies, remote signals or barrier semaphores. Data moves between devices by JAX's collectives and lax.ppermute only.
A program may use at most 256 MiB of HBM per device.

v0:
```python
import jax
import jax.numpy as jnp
from jax import lax
from jax.sharding import PartitionSpec as P

DH = 64
epsilon = 1e-05
masked_score = -1000000000.0
precise = lax.Precision.HIGHEST
LANES = 128


def layer_norm(values):
    centred = values - jnp.mean(values, axis=-1, keepdims=True)
    inv_std = lax.rsqrt(jnp.mean(centred * centred, axis=-1, keepdims=True) + epsilon)
    return (centred * inv_std, inv_std)


def norm_back(normed, inv_std, grad):
    mean_grad = jnp.mean(grad, axis=-1, keepdims=True)
    mean_proj = jnp.mean(grad * normed, axis=-1, keepdims=True)
    return inv_std * (grad - mean_grad - normed * mean_proj)


def silu_slope(values):
    sigma = jax.nn.sigmoid(values)
    return sigma * (1.0 + values * (1.0 - sigma))


def head_split(values):
    return values.reshape(values.shape[:-1] + (values.shape[-1] // DH, DH))


def swap_heads(values):
    return lax.ppermute(values, "head", [(0, 1), (1, 0)])


def whole_rows(own, first):
    other = swap_heads(own)
    return jnp.where(
        first, jnp.concatenate([own, other], axis=1), jnp.concatenate([other, own], axis=1)
    )


def own_rows(values, head, rows):
    return lax.dynamic_slice_in_dim(values, head * rows, rows, 1)


def head_sum(part):
    return part + swap_heads(part)


def attn_scores(queries, keys, biases, valid):
    scores = jnp.einsum("cqhe,ckhe->chqk", queries, keys, preferred_element_type=jnp.float32)
    scores = scores * DH ** (-0.5) + biases.astype(jnp.float32)
    return jnp.where(valid[:, None, None, :], scores, masked_score)


def to_chunks(values, parts):
    return values.reshape(parts, -1, LANES)


def shards(
    layer_input,
    pair_input,
    time_cond,
    chain_lengths,
    residue_mask,
    mod_weight,
    mod_bias,
    qkv_weight,
    pair_gain,
    pair_weight,
    out_weight,
    out_bias,
    gate_up_weight,
    down_weight,
    output_grad,
):
    chains = layer_input.shape[0]
    rows = layer_input.shape[1]
    width = layer_input.shape[2]
    length = residue_mask.shape[1]
    head = lax.axis_index("head")
    first = head == 0
    data_count = lax.axis_size("dp")
    x_rows = whole_rows(layer_input, first)
    g_rows = whole_rows(output_grad, first)
    positions = jnp.arange(length, dtype=jnp.int32)
    valid = (positions[None, :] < chain_lengths[:, None]) & (
        (residue_mask == 1) | (positions[None, :] == 0)
    )
    silu_cond = jax.nn.silu(time_cond).astype(jnp.bfloat16)
    modulation = jnp.dot(silu_cond, mod_weight, preferred_element_type=jnp.float32) + mod_bias
    scale_a, shift_a, gate_a, scale_t, shift_t, gate_t = [
        modulation[:, None, section * width : (section + 1) * width] for section in range(6)
    ]
    pair_norm, pair_inv = layer_norm(pair_input.astype(jnp.float32))
    pair_normed = (pair_norm * pair_gain).astype(jnp.bfloat16)
    bias_rows = jnp.einsum(
        "cqkp,ph->chqk", pair_normed, pair_weight, preferred_element_type=jnp.float32
    ).astype(jnp.bfloat16)
    biases = lax.all_to_all(bias_rows, "head", split_axis=1, concat_axis=2, tiled=True)
    residues = x_rows.astype(jnp.float32)
    norm_in, inv_in = layer_norm(residues)
    normed_a = (norm_in * (1.0 + scale_a) + shift_a).astype(jnp.bfloat16)
    projected = jnp.einsum(
        "cld,dtf->tclf", normed_a, qkv_weight, preferred_element_type=jnp.float32
    ).astype(jnp.bfloat16)
    queries = head_split(projected[0])
    keys = head_split(projected[1])
    values = head_split(projected[2])
    scores = attn_scores(queries, keys, biases, valid)
    row_max = jnp.max(scores, axis=-1, keepdims=True)
    exp_scores = jnp.exp(scores - row_max)
    row_total = jnp.sum(exp_scores, axis=-1, keepdims=True)
    attn_probs = exp_scores / row_total
    probs_low = attn_probs.astype(jnp.bfloat16)
    mixed = jnp.einsum("chqk,ckhe->cqhe", probs_low, values, preferred_element_type=jnp.float32)
    mixed = mixed.reshape(mixed.shape[:2] + (-1,)).astype(jnp.bfloat16)
    attn_part = jnp.einsum("clf,fd->cld", mixed, out_weight, preferred_element_type=jnp.float32)
    attn_branch = head_sum(attn_part) + out_bias
    sig_a = jax.nn.sigmoid(gate_a)
    middle = residues + sig_a * attn_branch
    norm_mid, inv_mid = layer_norm(middle)
    normed_t = (norm_mid * (1.0 + scale_t) + shift_t).astype(jnp.bfloat16)
    gate_up = jnp.einsum(
        "cld,dtf->tclf", normed_t, gate_up_weight, preferred_element_type=jnp.float32
    )
    hidden = (jax.nn.silu(gate_up[0]) * gate_up[1]).astype(jnp.bfloat16)
    ffn_part = jnp.einsum(
        "clf,fd->cld", hidden, down_weight, preferred_element_type=jnp.float32
    ).astype(jnp.bfloat16)
    ffn_branch = ffn_part.astype(jnp.float32) + swap_heads(ffn_part).astype(jnp.float32)
    sig_t = jax.nn.sigmoid(gate_t)
    layer_output = own_rows((middle + sig_t * ffn_branch).astype(jnp.bfloat16), head, rows)
    grad_out = g_rows.astype(jnp.float32)
    d_ffn = (grad_out * sig_t).astype(jnp.bfloat16)
    d_gate_t = jnp.sum(grad_out * ffn_branch * sig_t * (1.0 - sig_t), axis=1)
    down_grad_t = jnp.einsum("cld,clf->df", d_ffn, hidden, preferred_element_type=jnp.float32)
    d_hidden = jnp.einsum("cld,fd->clf", d_ffn, down_weight, preferred_element_type=jnp.float32)
    d_gate = d_hidden * gate_up[1] * silu_slope(gate_up[0])
    d_up = d_hidden * jax.nn.silu(gate_up[0])
    d_gate_up = jnp.stack([d_gate, d_up]).astype(jnp.bfloat16)
    gate_up_grad = jnp.einsum(
        "cld,tclf->dtf", normed_t, d_gate_up, preferred_element_type=jnp.float32
    )
    ffn_in_part = jnp.einsum(
        "tclf,dtf->cld", d_gate_up, gate_up_weight, preferred_element_type=jnp.float32
    )
    d_normed_t = head_sum(ffn_in_part)
    d_middle = grad_out + norm_back(norm_mid, inv_mid, d_normed_t * (1.0 + scale_t))
    d_scale_t = jnp.sum(d_normed_t * norm_mid, axis=1)
    d_shift_t = jnp.sum(d_normed_t, axis=1)
    d_attn = d_middle * sig_a
    d_gate_a = jnp.sum(d_middle * attn_branch * sig_a * (1.0 - sig_a), axis=1)
    d_out_bias = jnp.sum(d_attn, axis=(0, 1))
    d_attn_low = d_attn.astype(jnp.bfloat16)
    out_weight_grad_t = jnp.einsum(
        "cld,clf->df", d_attn_low, mixed, preferred_element_type=jnp.float32
    )
    d_mixed = head_split(
        jnp.einsum(
            "cld,fd->clf", d_attn_low, out_weight, preferred_element_type=jnp.float32
        ).astype(jnp.bfloat16)
    )
    d_values = jnp.einsum("chqk,cqhe->ckhe", probs_low, d_mixed, preferred_element_type=jnp.float32)
    d_probs = jnp.einsum("cqhe,ckhe->chqk", d_mixed, values, preferred_element_type=jnp.float32)
    d_scores = (
        attn_probs * (d_probs - jnp.sum(d_probs * attn_probs, axis=-1, keepdims=True))
    ).astype(jnp.bfloat16)
    d_queries = jnp.einsum(
        "chqk,ckhe->cqhe", d_scores, keys, preferred_element_type=jnp.float32
    ) * DH ** (-0.5)
    d_keys = jnp.einsum(
        "chqk,cqhe->ckhe", d_scores, queries, preferred_element_type=jnp.float32
    ) * DH ** (-0.5)
    d_qkv = (
        jnp.stack([d_queries, d_keys, d_values]).reshape(3, chains, length, -1).astype(jnp.bfloat16)
    )
    qkv_grad = jnp.einsum("cld,tclf->dtf", normed_a, d_qkv, preferred_element_type=jnp.float32)
    packed = jnp.concatenate(
        [
            to_chunks(qkv_grad, data_count),
            to_chunks(out_weight_grad_t, data_count),
            to_chunks(gate_up_grad, data_count),
            to_chunks(down_grad_t, data_count),
        ],
        axis=1,
    ).astype(jnp.bfloat16)
    reduced = lax.psum_scatter(packed, "dp", scatter_dimension=0, tiled=True)[0].astype(jnp.float32)
    attn_in_part = jnp.einsum(
        "tclf,dtf->cld", d_qkv, qkv_weight, preferred_element_type=jnp.float32
    ).astype(jnp.bfloat16)
    d_normed_a = attn_in_part.astype(jnp.float32) + swap_heads(attn_in_part).astype(jnp.float32)
    input_grad = own_rows(
        d_middle + norm_back(norm_in, inv_in, d_normed_a * (1.0 + scale_a)), head, rows
    )
    d_scale_a = jnp.sum(d_normed_a * norm_in, axis=1)
    d_shift_a = jnp.sum(d_normed_a, axis=1)
    d_modulation = jnp.concatenate(
        [d_scale_a, d_shift_a, d_gate_a, d_scale_t, d_shift_t, d_gate_t], axis=-1
    )
    d_bias_rows = lax.all_to_all(d_scores, "head", split_axis=2, concat_axis=1, tiled=True)
    pair_weight_grad = jnp.einsum(
        "cqkp,chqk->ph", pair_normed, d_bias_rows, preferred_element_type=jnp.float32
    )
    d_pair_normed = jnp.einsum(
        "chqk,ph->cqkp", d_bias_rows, pair_weight, preferred_element_type=jnp.float32
    )
    pair_gain_grad = jnp.sum(d_pair_normed * pair_norm, axis=(0, 1, 2))
    pair_grad = norm_back(pair_norm, pair_inv, d_pair_normed * pair_gain).astype(jnp.bfloat16)
    pair_small = head_sum(jnp.concatenate([pair_weight_grad.reshape(-1), pair_gain_grad])[None])
    small = jnp.concatenate([d_modulation, time_cond, pair_small, d_out_bias[None]], axis=-1)
    small_rows = lax.all_gather(small, "dp", axis=0, tiled=True)
    mod_size = d_modulation.shape[-1]
    cond_size = time_cond.shape[-1]
    pw_size = pair_weight.size
    pg_size = pair_gain.size
    mod_chain = small_rows[:, :mod_size]
    cond_chain = small_rows[:, mod_size : mod_size + cond_size]
    rest = jnp.sum(small_rows[:, mod_size + cond_size :], axis=0)
    pair_weight_grad = rest[:pw_size].reshape(pair_weight.shape)
    pair_gain_grad = rest[pw_size : pw_size + pg_size]
    out_bias_grad = rest[pw_size + pg_size :]
    cond_act = lax.optimization_barrier(jax.nn.silu(cond_chain).astype(jnp.bfloat16)).astype(
        jnp.float32
    )
    mod_weight_grad = jnp.dot(cond_act.T, mod_chain, precision=precise)
    mod_bias_grad = jnp.sum(mod_chain, axis=0)
    cond_grad = jnp.dot(
        d_modulation, mod_weight.astype(jnp.float32).T, precision=precise
    ) * silu_slope(time_cond)
    sizes = [
        qkv_grad.size // data_count,
        out_weight_grad_t.size // data_count,
        gate_up_grad.size // data_count,
        down_grad_t.size // data_count,
    ]
    flat = reduced.reshape(-1)
    offsets = [0]
    for size in sizes:
        offsets.append(offsets[-1] + size)
    pieces = [flat[offsets[i] : offsets[i + 1]] for i in range(4)]
    qkv_grad = pieces[0].reshape((-1,) + qkv_grad.shape[1:])
    out_weight_grad = pieces[1].reshape(-1, out_weight_grad_t.shape[1]).T
    gate_up_grad = pieces[2].reshape((-1,) + gate_up_grad.shape[1:])
    down_grad = pieces[3].reshape(-1, down_grad_t.shape[1]).T
    return (
        layer_output,
        input_grad,
        pair_grad,
        cond_grad,
        mod_weight_grad,
        mod_bias_grad,
        qkv_grad,
        pair_gain_grad,
        pair_weight_grad,
        out_weight_grad,
        out_bias_grad,
        gate_up_grad,
        down_grad,
    )


def solution(mesh):
    placed = (
        P("dp", "head", None),
        P("dp", "head", None, None),
        P("dp", None),
        P("dp"),
        P("dp", None),
        P(),
        P(),
        P(None, None, "head"),
        P(),
        P(),
        P("head", None),
        P(),
        P(None, None, "head"),
        P("head", None),
        P("dp", "head", None),
    )
    return jax.shard_map(
        shards,
        mesh=mesh,
        in_specs=placed,
        out_specs=(
            P("dp", "head", None),
            P("dp", "head", None),
            P("dp", "head", None, None),
            P("dp", None),
            P(),
            P(),
            P("dp", None, "head"),
            P(),
            P(),
            P("head", "dp"),
            P(),
            P("dp", None, "head"),
            P("head", "dp"),
        ),
        check_vma=False,
    )
```

profile of v0, /device:TPU:0, one launch (start us, length us, event | category | flops | bytes accessed | tf_op | source)
XLA Modules:
  0.0 375.7 jit_solution(14148207465790848436)
XLA Ops:
  7.2 3.0 collective-permute-start
  10.2 22.4 %copy.116 = bf16[1,128,256,256]{2,3,1,0:T(8,128)(2,1)} copy(bf16[1,128,256,256]{3,2,1,0:T(8,128)(2,1)} %param.16) | data formatting | bytes 33554432 | tf_op args[1]
  32.6 6.9 %convert_reduce_fusion = f32[128,256]{1,0:T(8,128)S(1)} fusion(bf16[1,128,256,256]{2,3,1,0:T(8,128)(2,1)} %copy.116), kind=kLoop, calls=%fused_computation.2 | loop fusion | flops 16744448 | bytes 16908288 | tf_op jit(solution)/shard_map/reduce_sum | solution.py:14
  39.5 3.7 copy-done.2
  43.3 4.7 %fusion.13 = f32[128,256]{1,0:T(8,128)S(1)} fusion(bf16[1,128,256,256]{2,3,1,0:T(8,128)(2,1)S(1)} %copy-done.2, f32[128,256]{1,0:T(8,128)S(1)} %broadcast_multiply_fusion.2), kind=kLoop, calls=%fused_computation.15 | loop fusion | flops 33521664 | bytes 17039360 | tf_op jit(solution)/shard_map/reduce_sum | solution.py:15
  48.0 5.2 %fusion.39 = bf16[1,12,128,256]{3,1,2,0:T(8,128)(2,1)S(1)} fusion(bf16[1,128,256,256]{2,3,1,0:T(8,128)(2,1)S(1)} %copy-done.2, f32[256]{0:T(256)S(1)} %copy-done.52, f32[128,256]{1,0:T(8,128)S(1)} %add_rsqrt_fusion, f32[128,256]{1,0:T(8,128)S(1)} %broadcast_multiply_fusion.2, bf16[256,12]{0,1:T(8,128)(2,1)S(1)} %copy-done.61), kind=kOutput, calls=%fused_computation.52 | convolution fusion | flops 243662848 | bytes 17832960 | tf_op jit(solution)/shard_map/cqkp,ph->chqk/dot_general | solution.py:100
  54.4 3.7 all-to-all-start
  73.6 3.7 copy.120
  77.3 3.4 reshape.1017
  85.2 3.1 convolution_convert_fusion.8
  92.5 17.9 %collective-permute-done.1 = f32[1,256,768]{2,1,0:T(8,128)} collective-permute-done((f32[1,256,768]{2,1,0:T(8,128)S(1)}, f32[1,256,768]{2,1,0:T(8,128)}, u32[]{:S(2)}, u32[]{:S(2)}) %collective-permute-start.1) | collective-permute-done | bytes 786464 | tf_op jit(solution)/shard_map/ppermute | solution.py:35
  112.3 4.0 %fusion.19 = f32[2,1,256,1536]{3,2,0,1:T(8,128)S(1)} fusion(bf16[768,2,1536]{2,1,0:T(2,128)(2,1)} %param.27, f32[1,256,768]{2,1,0:T(8,128)S(1)} %get-tuple-element.87, f32[768]{0:T(1024)} %get-tuple-element.78, f32[768]{0:T(1024)S(1)} %get-tuple-element.79, f32[256]{0:T(256)S(1)} %add_rsqrt_fusion.1, f32[256]{0:T(256)S(1)} %broadcast_multiply_fusion.7), kind=kOutput, calls=%fused_computation.25 | convolution fusion | flops 1208942592 | bytes 8658944 | tf_op jit(solution)/shard_map/cld,dtf->tclf/dot_general | solution.py:127
  123.4 3.4 convolution_convert_fusion.1
  126.8 5.8 %reshape.1011 = bf16[16,576,128]{2,1,0:T(8,128)(2,1)} reshape(bf16[768,1536]{1,0:T(8,128)(2,1)} %convolution_convert_fusion.1) | data formatting | bytes 4718592 | tf_op jit(solution)/shard_map/reshape | solution.py:60
  132.6 5.1 %convolution_convert_fusion = bf16[768,2,1536]{2,0,1:T(8,128)(2,1)} fusion(bf16[1,256,1536]{2,1,0:T(8,128)(2,1)} %copy-done.23, bf16[1,256,1536]{2,1,0:T(8,128)(2,1)} %copy-done.22, f32[1,256,768]{2,1,0:T(8,128)S(1)} %get-tuple-element.87, f32[768]{0:T(1024)} %get-tuple-element.78, f32[768]{0:T(1024)S(1)} %get-tuple-element.79, f32[256]{0:T(256)} %copy-done.46, ...), kind=kOutput, calls=%fused_computation.19 | convolution fusion | flops 1214447616 | bytes 7086080 | tf_op jit(solution)/shard_map/cld,tclf->dtf/dot_general | solution.py:145
  137.7 9.3 %copy.141 = bf16[768,2,1536]{2,1,0:T(2,128)(2,1)} copy(bf16[768,2,1536]{2,0,1:T(8,128)(2,1)} %convolution_convert_fusion) | data formatting | bytes 9437184 | tf_op jit(solution)/shard_map/convert.10
  147.0 11.4 %reshape.1010 = bf16[16,1152,128]{2,1,0:T(8,128)(2,1)} reshape(bf16[768,2,1536]{2,1,0:T(2,128)(2,1)} %copy.141) | data formatting | bytes 9437184 | tf_op jit(solution)/shard_map/reshape | solution.py:60
  167.6 3.2 convolution_convert_fusion.6
  185.3 2.9 copy.139
  188.3 5.4 %reshape.1008 = bf16[16,432,128]{2,1,0:T(8,128)(2,1)} reshape(bf16[768,3,384]{2,1,0:T(4,128)(2,1)} %copy.139) | data formatting | bytes 3538944 | tf_op jit(solution)/shard_map/reshape | solution.py:60
  193.6 7.5 %pad_maximum_fusion = bf16[16,2304,128]{2,1,0:T(8,128)(2,1)} fusion(bf16[16,576,128]{2,1,0:T(8,128)(2,1)} %reshape.1011, bf16[16,1152,128]{2,1,0:T(8,128)(2,1)} %reshape.1010, bf16[16,144,128]{2,1,0:T(8,128)(2,1)} %reshape.1009, bf16[16,432,128]{2,1,0:T(8,128)(2,1)} %reshape.1008), kind=kLoop, calls=%fused_computation.18 | loop fusion | flops 37748736 | bytes 18874368 | tf_op jit(solution)/shard_map/concatenate | solution.py:182
  201.2 3.0 fusion.48
  207.7 8.2 %collective-permute-done.2 = bf16[1,256,768]{2,1,0:T(8,128)(2,1)S(1)} collective-permute-done((bf16[1,256,768]{2,1,0:T(8,128)(2,1)S(1)}, bf16[1,256,768]{2,1,0:T(8,128)(2,1)S(1)}, u32[]{:S(2)}, u32[]{:S(2)}) %collective-permute-start.2) | collective-permute-done | bytes 393248 | tf_op jit(solution)/shard_map/ppermute | solution.py:35
  219.8 3.6 all-to-all-start.1
  226.1 6.8 %all-to-all-done.1 = bf16[1,6,256,256]{3,1,0,2:T(8,128)(2,1)S(1)} async-done(((bf16[1,6,256,256]{3,1,0,2:T(8,128)(2,1)}), bf16[1,6,256,256]{3,1,0,2:T(8,128)(2,1)S(1)}, u32[]{:S(2)}, u32[]{:S(2)}) %all-to-all-start.1) | async-done | bytes 786464 | tf_op jit(solution)/shard_map/all_to_all | solution.py:204
  233.1 10.0 %fusion.51 = f32[256,12]{1,0:T(8,128)S(1)} fusion(bf16[1,128,256,256]{2,3,1,0:T(8,128)(2,1)} %copy.116, f32[256]{0:T(256)S(1)} %copy-done.53, f32[128,256]{1,0:T(8,128)S(1)} %copy-done.29, f32[128,256]{1,0:T(8,128)S(1)} %copy-done.21, bf16[12,128,256]{2,1,0:T(8,128)(2,1)S(1)} %bitcast.217), kind=kOutput, calls=%fused_computation.73 | convolution fusion | flops 243269632 | bytes 17839104 | tf_op jit(solution)/shard_map/cqkp,chqk->ph/dot_general | solution.py:205
  243.3 21.5 %fusion.12 = (f32[256]{0:T(256)S(1)}, f32[128,256]{1,0:T(8,128)S(1)}, f32[128,256,256]{1,2,0:T(8,128)}) fusion(bf16[1,128,256,256]{2,3,1,0:T(8,128)(2,1)} %copy.116, f32[128,256]{1,0:T(8,128)S(1)} %copy-done.29, f32[128,256]{1,0:T(8,128)S(1)} %copy-done.21, f32[256]{0:T(256)S(1)} %copy-done.53, bf16[256,12]{0,1:T(8,128)(2,1)S(1)} %copy-done.62, ...), kind=kOutput, calls=%fused_computation.14 | convolution fusion | flops 268402432 | bytes 51519488 | tf_op jit(solution)/shard_map/chqk,ph->cqkp/dot_general | solution.py:208
  265.4 15.1 %multiply_reduce_fusion = f32[128,256]{1,0:T(8,128)S(1)} fusion(f32[128,256,256]{1,2,0:T(8,128)} %get-tuple-element.115, f32[256]{0:T(256)S(1)} %copy-done.53), kind=kLoop, calls=%fused_computation.16 | loop fusion | flops 16744448 | bytes 33686528 | tf_op jit(solution)/shard_map/reduce_sum | solution.py:20
  284.0 24.9 %fusion.11 = bf16[1,128,256,256]{2,3,1,0:T(8,128)(2,1)} fusion(bf16[1,128,256,256]{2,3,1,0:T(8,128)(2,1)} %copy.116, f32[128,256,256]{1,2,0:T(8,128)} %get-tuple-element.115, f32[128,256]{1,0:T(8,128)S(1)} %broadcast_multiply_fusion, f32[128,256]{1,0:T(8,128)S(1)} %broadcast_multiply_fusion.1, f32[256]{0:T(256)S(1)} %copy-done.53, ...), kind=kLoop, calls=%fused_computation.13 | loop fusion | flops 75497472 | bytes 67634176 | tf_op jit(solution)/shard_map/convert_element_type | solution.py:212
  308.9 22.4 %copy.142 = bf16[1,128,256,256]{3,2,1,0:T(8,128)(2,1)} copy(bf16[1,128,256,256]{2,3,1,0:T(8,128)(2,1)} %fusion.11) | data formatting | bytes 33554432
  331.3 23.8 %all-gather = f32[16,1,8960]{2,1,0:T(1,128)S(1)} all-gather(f32[1,1,8960]{2,1,0:T(1,128)S(1)} %bitcast.228), channel_id=1, replica_groups=mesh['dp'=16,'head'=2] {'dp'}, dimensions={0}, use_global_device_ids=true | all-gather | bytes 609280 | tf_op jit(solution)/shard_map/all_gather | solution.py:215
  357.9 4.2 %fusion.77 = f32[256,4608]{1,0:T(8,128)} fusion(bf16[16,256]{1,0:T(8,128)(2,1)S(1)} %multiply_convert_fusion.8, f32[16,8960]{1,0:T(8,128)S(1)} %bitcast.202), kind=kOutput, calls=%fused_computation.129 | convolution fusion | flops 226492416 | bytes 5021696 | tf_op jit(solution)/shard_map/dot_general | solution.py:229
  (237 shorter events, 80.6 us)
Async XLA Ops:
  7.2 109.2 %copy-start = (bf16[1536,768]{1,0:T(8,128)(2,1)S(1)}, bf16[1536,768]{1,0:T(8,128)(2,1)}, u32[]{:S(2)}) copy-start(bf16[1536,768]{1,0:T(8,128)(2,1)} %param.28) | copy-start | bytes 7077892
  7.2 56.3 %collective-permute-start = (bf16[1,128,768]{2,1,0:T(8,128)(2,1)}, bf16[1,128,768]{2,1,0:T(8,128)(2,1)S(1)}, u32[]{:S(2)}, u32[]{:S(2)}) collective-permute-start(bf16[1,128,768]{2,1,0:T(8,128)(2,1)} %param.15), channel_id=1, source_target_pairs={{0,1},{1,0},{2,3},{3,2},{4,5},{5,4},{6,7},{7,6},{8,9},{9,8},{10,11... | collective-permute-start | bytes 589832 | tf_op jit(solution)/shard_map/ppermute | solution.py:35
  32.6 10.7 %copy-start.2 = (bf16[1,128,256,256]{2,3,1,0:T(8,128)(2,1)S(1)}, bf16[1,128,256,256]{2,3,1,0:T(8,128)(2,1)}, u32[]{:S(2)}) copy-start(bf16[1,128,256,256]{2,3,1,0:T(8,128)(2,1)} %copy.116) | copy-start | bytes 50331652
  54.4 7.7 %copy-start.58 = (s32[1,256]{1,0:T(1,128)S(1)}, s32[1,256]{1,0:T(1,128)}, u32[]{:S(2)}) copy-start(s32[1,256]{1,0:T(1,128)} %param.19) | copy-start | bytes 3076
  54.4 9.1 %copy-start.12 = (bf16[1,128,768]{2,1,0:T(8,128)(2,1)S(1)}, bf16[1,128,768]{2,1,0:T(8,128)(2,1)}, u32[]{:S(2)}) copy-start(bf16[1,128,768]{2,1,0:T(8,128)(2,1)} %param.15) | copy-start | bytes 589828
  54.4 17.9 %all-to-all-start = ((bf16[1,12,128,256]{3,2,0,1:T(8,128)(2,1)}), bf16[1,12,128,256]{3,2,0,1:T(8,128)(2,1)S(1)}, u32[]{:S(2)}, u32[]{:S(2)}) async-start(bf16[1,12,128,256]{3,2,0,1:T(8,128)(2,1)} %copy.118), calls=%async_computation | async-start | bytes 1572864 | tf_op jit(solution)/shard_map/all_to_all | solution.py:103
  58.0 304.0 %reduce-scatter.2.cloned.1.call-start = ((), (), s32[]{:S(2)}) async-start(), calls=%async_computation.3 | async-start | bytes 10027008 | tf_op jit(solution)/shard_map/reduce_scatter | solution.py:191
  85.2 25.3 %copy-start.41 = (f32[768]{0:T(1024)S(1)}, f32[768]{0:T(1024)}, u32[]{:S(2)}) copy-start(f32[768]{0:T(1024)} %param.26) | copy-start | bytes 9220
  89.8 20.6 %collective-permute-start.1 = (f32[1,256,768]{2,1,0:T(8,128)S(1)}, f32[1,256,768]{2,1,0:T(8,128)}, u32[]{:S(2)}, u32[]{:S(2)}) collective-permute-start(f32[1,256,768]{2,1,0:T(8,128)S(1)} %convolution_bitcast_fusion), channel_id=1, source_target_pairs={{0,1},{1,0},{2,3},{3,2},{4,5},{5,4},{6,7},{7,6},{8,9},{9,8},{10,11... | collective-permute-start | bytes 2359304 | tf_op jit(solution)/shard_map/ppermute | solution.py:35
  91.9 24.5 %collective-permute-start.3 = (bf16[1,128,768]{2,1,0:T(8,128)(2,1)}, bf16[1,128,768]{2,1,0:T(8,128)(2,1)}, u32[]{:S(2)}, u32[]{:S(2)}) collective-permute-start(bf16[1,128,768]{2,1,0:T(8,128)(2,1)} %param.29), channel_id=1, source_target_pairs={{0,1},{1,0},{2,3},{3,2},{4,5},{5,4},{6,7},{7,6},{8,9},{9,8},{10,11... | collective-permute-start | bytes 589832 | tf_op jit(solution)/shard_map/ppermute | solution.py:35
  121.5 37.0 %collective-permute-start.4 = (f32[1,256,768]{2,1,0:T(8,128)}, f32[1,256,768]{2,1,0:T(8,128)}, u32[]{:S(2)}, u32[]{:S(2)}) collective-permute-start(f32[1,256,768]{2,1,0:T(8,128)} %fusion.42), channel_id=1, source_target_pairs={{0,1},{1,0},{2,3},{3,2},{4,5},{5,4},{6,7},{7,6},{8,9},{9,8},{10,11... | collective-permute-start | bytes 2359304 | tf_op jit(solution)/shard_map/ppermute | solution.py:35
  173.8 9.5 %copy-start.40 = (f32[768]{0:T(1024)S(1)}, f32[768]{0:T(1024)}, u32[]{:S(2)}) copy-start(f32[768]{0:T(1024)} %copy-done.39) | copy-start | bytes 9220
  173.8 9.5 %copy-start.51 = (f32[256]{0:T(256)S(1)}, f32[256]{0:T(256)}, u32[]{:S(2)}) copy-start(f32[256]{0:T(256)} %copy-done.50) | copy-start | bytes 3076
  173.8 9.5 %copy-start.55 = (f32[256]{0:T(256)S(1)}, f32[256]{0:T(256)}, u32[]{:S(2)}) copy-start(f32[256]{0:T(256)} %copy-done.54) | copy-start | bytes 3076
  204.2 11.8 %copy-start.27 = (bf16[1,128,768]{2,1,0:T(8,128)(2,1)S(1)}, bf16[1,128,768]{2,1,0:T(8,128)(2,1)}, u32[]{:S(2)}) copy-start(bf16[1,128,768]{2,1,0:T(8,128)(2,1)} %param.29) | copy-start | bytes 589828
  204.2 11.7 %collective-permute-start.2 = (bf16[1,256,768]{2,1,0:T(8,128)(2,1)S(1)}, bf16[1,256,768]{2,1,0:T(8,128)(2,1)S(1)}, u32[]{:S(2)}, u32[]{:S(2)}) collective-permute-start(bf16[1,256,768]{2,1,0:T(8,128)(2,1)S(1)} %fusion.48), channel_id=1, source_target_pairs={{0,1},{1,0},{2,3},{3,2},{4,5},{5,4},{6,7},{7,6},{8,9},{9,8},{10,11... | collective-permute-start | bytes 1179656 | tf_op jit(solution)/shard_map/ppermute | solution.py:35
  205.7 12.4 %copy-start.4 = (bf16[6,256,256]{1,2,0:T(8,128)(2,1)S(1)}, bf16[6,256,256]{1,2,0:T(8,128)(2,1)}, u32[]{:S(2)}) copy-start(bf16[6,256,256]{1,2,0:T(8,128)(2,1)} %copy-done.3) | copy-start | bytes 2359300
  205.7 17.8 %collective-permute-start.5 = (bf16[1,256,768]{2,1,0:T(8,128)(2,1)S(1)}, bf16[1,256,768]{2,1,0:T(8,128)(2,1)}, u32[]{:S(2)}, u32[]{:S(2)}) collective-permute-start(bf16[1,256,768]{2,1,0:T(8,128)(2,1)S(1)} %fusion.47), channel_id=1, source_target_pairs={{0,1},{1,0},{2,3},{3,2},{4,5},{5,4},{6,7},{7,6},{8,9},{9,8},{10,11... | collective-permute-start | bytes 1179656 | tf_op jit(solution)/shard_map/ppermute | solution.py:35
  219.8 13.0 %all-to-all-start.1 = ((bf16[1,6,256,256]{3,1,0,2:T(8,128)(2,1)}), bf16[1,6,256,256]{3,1,0,2:T(8,128)(2,1)S(1)}, u32[]{:S(2)}, u32[]{:S(2)}) async-start(bf16[1,6,256,256]{3,1,0,2:T(8,128)(2,1)} %copy.131), calls=%async_computation.1 | async-start | bytes 2097152 | tf_op jit(solution)/shard_map/all_to_all | solution.py:204
  225.9 7.2 %copy-start.29 = (f32[128,256]{1,0:T(8,128)S(1)}, f32[128,256]{1,0:T(8,128)}, u32[]{:S(2)}) copy-start(f32[128,256]{1,0:T(8,128)} %copy-done.28) | copy-start | bytes 393220
  225.9 7.2 %copy-start.53 = (f32[256]{0:T(256)S(1)}, f32[256]{0:T(256)}, u32[]{:S(2)}) copy-start(f32[256]{0:T(256)} %param.23) | copy-start | bytes 3076
  233.1 10.1 %copy-start.62 = (bf16[256,12]{0,1:T(8,128)(2,1)S(1)}, bf16[256,12]{0,1:T(8,128)(2,1)}, u32[]{:S(2)}) copy-start(bf16[256,12]{0,1:T(8,128)(2,1)} %param.24) | copy-start | bytes 18436
  243.2 22.0 %copy-start.44 = (f32[768]{0:T(1024)S(1)}, f32[768]{0:T(1024)}, u32[]{:S(2)}) copy-start(f32[768]{0:T(1024)} %get-tuple-element.71) | copy-start | bytes 9220
  243.2 22.0 %copy-start.38 = (f32[768]{0:T(1024)S(1)}, f32[768]{0:T(1024)}, u32[]{:S(2)}) copy-start(f32[768]{0:T(1024)} %get-tuple-element.67) | copy-start | bytes 9220
  243.2 22.0 %copy-start.37 = (f32[768]{0:T(1024)S(1)}, f32[768]{0:T(1024)}, u32[]{:S(2)}) copy-start(f32[768]{0:T(1024)} %get-tuple-element.72) | copy-start | bytes 9220
  264.8 66.5 %collective-permute-start.6 = (f32[1,3328]{1,0:T(1,128)S(1)}, f32[1,3328]{1,0:T(1,128)S(1)}, u32[]{:S(2)}, u32[]{:S(2)}) collective-permute-start(f32[1,3328]{1,0:T(1,128)S(1)} %broadcast_in_dim.17), channel_id=1, source_target_pairs={{0,1},{1,0},{2,3},{3,2},{4,5},{5,4},{6,7},{7,6},{8,9},{9,8},{10,11... | collective-permute-start | bytes 39944 | tf_op jit(solution)/shard_map/ppermute | solution.py:35
  265.3 15.2 %copy-start.6 = (f32[1,256,768]{2,1,0:T(8,128)S(1)}, f32[1,256,768]{2,1,0:T(8,128)}, u32[]{:S(2)}) copy-start(f32[1,256,768]{2,1,0:T(8,128)} %copy-done.5) | copy-start | bytes 2359300
  265.3 15.2 %copy-start.15 = (f32[1,256,768]{2,1,0:T(8,128)S(1)}, f32[1,256,768]{2,1,0:T(8,128)}, u32[]{:S(2)}) copy-start(f32[1,256,768]{2,1,0:T(8,128)} %get-tuple-element.98) | copy-start | bytes 2359300
  265.4 15.2 %copy-start.59 = (f32[128]{0:T(128)S(1)}, f32[128]{0:T(128)}, u32[]{:S(2)}) copy-start(f32[128]{0:T(128)} %dynamic-slice.2) | copy-start | bytes 1540
  265.4 16.1 %copy-start.7 = (bf16[256,4608]{1,0:T(8,128)(2,1)S(1)}, bf16[256,4608]{1,0:T(8,128)(2,1)}, u32[]{:S(2)}) copy-start(bf16[256,4608]{1,0:T(8,128)(2,1)} %param.20) | copy-start | bytes 7077892
  265.4 16.1 %copy-start.49 = (f32[1,256]{1,0:T(1,128)S(1)}, f32[1,256]{1,0:T(1,128)}, u32[]{:S(2)}) copy-start(f32[1,256]{1,0:T(1,128)} %param.17) | copy-start | bytes 3076
  308.9 22.4 %copy-start.43 = (f32[768]{0:T(1024)S(1)}, f32[768]{0:T(1024)}, u32[]{:S(2)}) copy-start(f32[768]{0:T(1024)} %get-tuple-element.70) | copy-start | bytes 9220
  (44 other events, 153.3 us)
Sparse Core Ops, SparseCore 0:
  201.3 111.5 reduce-scatter.1
where the time goes:
time: 382 us; the launch traced here: 376 us
  local copies, waits for them, and re-layouts  121 us (32%)
  matrix products  87 us (23%)
  other arithmetic  77.7 us (20%)
  waiting for transfers between devices  33 us (9%)
  blocking collectives  23.8 us (6%)
  starting transfers between devices  17.6 us (5%)
  between operations  16.1 us (4%)
    unnamed x144, local copies, waits for them, and re-layouts  52.1 us
    ppermute x7, waiting for transfers between devices, swap_heads(): return lax.ppermute(values, 'head', [(0, 1), (1, 0)])  26.1 us
    convert_element_type x1, other arithmetic, shards(): norm_back(pair_norm, pair_inv, d_pair_normed * pair_gain)  24.9 us
    reshape x4, local copies, waits for them, and re-layouts, to_chunks(): return values.reshape(parts, -1, LANES)  24.8 us
    all_gather x1, blocking collectives, shards(): small_rows = lax.all_gather(small, 'dp', axis=0, tiled=True)  23.8 us
    dot_general x1, matrix products, shards(): jnp.einsum('chqk,ph->cqkp', d_bias_rows, pair_weight, preferred_element_t...  21.5 us
    reduce_sum x1, other arithmetic, norm_back(): mean_grad = jnp.mean(grad, axis=-1, keepdims=True)  15.1 us
    another operation x2, local copies, waits for them, and re-layouts  12.2 us
  transfers between devices with their start and end apart: 10, of which 3 were waited for; matrix products, arithmetic and copies ran while one was open for 56% of the time, Pallas kernels for 0%

commit v1 on v0

--- a/solution.py
+++ b/solution.py
@@ -201,7 +201,10 @@
     d_modulation = jnp.concatenate(
         [d_scale_a, d_shift_a, d_gate_a, d_scale_t, d_shift_t, d_gate_t], axis=-1
     )
-    d_bias_rows = lax.all_to_all(d_scores, "head", split_axis=2, concat_axis=1, tiled=True)
+    d_bias_rows = jnp.concatenate(
+        lax.all_to_all(jnp.stack(jnp.split(d_scores, lax.axis_size("head"), axis=2)), "head", 0, 0),
+        axis=1,
+    )
     pair_weight_grad = jnp.einsum(
         "cqkp,chqk->ph", pair_normed, d_bias_rows, preferred_element_type=jnp.float32
     )

time: 382 us -> 357 us (0.935)
  waiting for transfers between devices: 33 us -> 24.2 us
  matrix products: 87 us -> 79.5 us
  local copies, waits for them, and re-layouts: 121 us -> 114 us
    ppermute x7, waiting for transfers between devices: 26.1 us -> 17.8 us  [swap_heads(): return lax.ppermute(values, 'head', [(0, 1), (1, 0)])]
    another operation x2 -> x4, local copies, waits for them, and re-layouts: 12.2 us -> 14.3 us
    unnamed x144 -> x138, local copies, waits for them, and re-layouts: 52.1 us -> 52.7 us
  transfers between devices with their start and end apart: 10 -> 10, of which waited for: 3 -> 2; matrix products, arithmetic and copies ran while one was open for 56% -> 69% of each run, Pallas kernels for 0% -> 0%
where the time goes in v1:
time: 357 us; the launch traced here: 351 us
  local copies, waits for them, and re-layouts  114 us (32%)
  matrix products  79.5 us (22%)
  other arithmetic  75.9 us (21%)
  waiting for transfers between devices  24.2 us (7%)
  blocking collectives  23.3 us (7%)
  starting transfers between devices  17.6 us (5%)
  between operations  16.1 us (5%)
    unnamed x138, local copies, waits for them, and re-layouts  52.7 us
    convert_element_type x1, other arithmetic, shards(): norm_back(pair_norm, pair_inv, d_pair_normed * pair_gain)  25.2 us
    all_gather x1, blocking collectives, shards(): small_rows = lax.all_gather(small, 'dp', axis=0, tiled=True)  23.3 us
    reshape x4, local copies, waits for them, and re-layouts, to_chunks(): return values.reshape(parts, -1, LANES)  22 us
    dot_general x1, matrix products, shards(): jnp.einsum('chqk,ph->cqkp', d_bias_rows, pair_weight, preferred_element_t...  21.7 us
    ppermute x7, waiting for transfers between devices, swap_heads(): return lax.ppermute(values, 'head', [(0, 1), (1, 0)])  17.8 us
    reduce_sum x1, other arithmetic, norm_back(): mean_grad = jnp.mean(grad, axis=-1, keepdims=True)  14.8 us
    another operation x3, local copies, waits for them, and re-layouts  14.1 us
  transfers between devices with their start and end apart: 10, of which 2 were waited for; matrix products, arithmetic and copies ran while one was open for 69% of the time, Pallas kernels for 0%

profile of v1, /device:TPU:0, one launch (start us, length us, event | category | flops | bytes accessed | tf_op | source)
XLA Modules:
  0.0 351.0 jit_solution(2505753306162809974)
XLA Ops:
  7.2 3.0 collective-permute-start
  10.2 22.4 %copy.85 = bf16[1,128,256,256]{2,3,1,0:T(8,128)(2,1)} copy(bf16[1,128,256,256]{3,2,1,0:T(8,128)(2,1)} %param.16) | data formatting | bytes 33554432 | tf_op args[1]
  32.6 6.9 %convert_reduce_fusion = f32[128,256]{1,0:T(8,128)S(1)} fusion(bf16[1,128,256,256]{2,3,1,0:T(8,128)(2,1)} %copy.85), kind=kLoop, calls=%fused_computation.2 | loop fusion | flops 16744448 | bytes 16908288 | tf_op jit(solution)/shard_map/reduce_sum | solution.py:14
  39.5 3.7 %copy-done.2 = bf16[1,128,256,256]{2,3,1,0:T(8,128)(2,1)S(1)} copy-done((bf16[1,128,256,256]{2,3,1,0:T(8,128)(2,1)S(1)}, bf16[1,128,256,256]{2,3,1,0:T(8,128)(2,1)}, u32[]{:S(2)}) %copy-start.2) | copy-done | bytes 16777240
  43.3 4.7 %fusion.13 = f32[128,256]{1,0:T(8,128)S(1)} fusion(bf16[1,128,256,256]{2,3,1,0:T(8,128)(2,1)S(1)} %copy-done.2, f32[128,256]{1,0:T(8,128)S(1)} %broadcast_multiply_fusion.2), kind=kLoop, calls=%fused_computation.15 | loop fusion | flops 33521664 | bytes 17039360 | tf_op jit(solution)/shard_map/reduce_sum | solution.py:15
  48.0 5.2 %fusion.39 = bf16[1,12,128,256]{3,1,2,0:T(8,128)(2,1)S(1)} fusion(bf16[1,128,256,256]{2,3,1,0:T(8,128)(2,1)S(1)} %copy-done.2, f32[256]{0:T(256)S(1)} %copy-done.51, f32[128,256]{1,0:T(8,128)S(1)} %add_rsqrt_fusion, f32[128,256]{1,0:T(8,128)S(1)} %broadcast_multiply_fusion.2, bf16[256,12]{0,1:T(8,128)(2,1)S(1)} %copy-done.59), kind=kOutput, calls=%fused_computation.52 | convolution fusion | flops 243662848 | bytes 17832960 | tf_op jit(solution)/shard_map/cqkp,ph->chqk/dot_general | solution.py:100
  54.4 3.7 %all-to-all-start = ((bf16[1,12,128,256]{3,2,0,1:T(8,128)(2,1)}), bf16[1,12,128,256]{3,2,0,1:T(8,128)(2,1)S(1)}, u32[]{:S(2)}, u32[]{:S(2)}) async-start(bf16[1,12,128,256]{3,2,0,1:T(8,128)(2,1)} %copy.87), calls=%async_computation | async-start | bytes 1572864 | tf_op jit(solution)/shard_map/all_to_all | solution.py:103
  73.6 3.7 %copy.89 = f32[1,6,2,128,256]{3,2,4,1,0:T(2,128)} copy(f32[1,6,2,128,256]{4,3,1,2,0:T(8,128)} %convert_bitcast_fusion) | data formatting | bytes 3145728 | tf_op jit(solution)/shard_map/convert_element_type | solution.py:55
  77.3 3.4 reshape.1018
  85.7 2.5 convolution_convert_fusion.8
  91.4 17.8 %collective-permute-done.1 = f32[1,256,768]{2,1,0:T(8,128)S(1)} collective-permute-done((f32[1,256,768]{2,1,0:T(8,128)S(1)}, f32[1,256,768]{2,1,0:T(8,128)S(1)}, u32[]{:S(2)}, u32[]{:S(2)}) %collective-permute-start.1) | collective-permute-done | bytes 786464 | tf_op jit(solution)/shard_map/ppermute | solution.py:35
  110.3 3.8 %fusion.19 = f32[2,1,256,1536]{3,2,0,1:T(8,128)S(1)} fusion(bf16[768,2,1536]{2,1,0:T(2,128)(2,1)} %param.27, f32[1,256,768]{2,1,0:T(8,128)S(1)} %get-tuple-element.74, f32[768]{0:T(1024)S(1)} %copy-done.38, f32[768]{0:T(1024)S(1)} %get-tuple-element.66, f32[256]{0:T(256)S(1)} %add_rsqrt_fusion.1, f32[256]{0:T(256)S(1)} %broadcast_multiply_fusion.7), kind=kOutput, calls=%fused_computation.25 | convolution fusion | flops 1208942592 | bytes 8658944 | tf_op jit(solution)/shard_map/cld,dtf->tclf/dot_general | solution.py:127
  122.5 3.9 %reshape.1012 = bf16[16,576,128]{2,1,0:T(8,128)(2,1)} reshape(bf16[768,1536]{1,0:T(8,128)(2,1)S(1)} %convolution_convert_fusion.1) | data formatting | bytes 4718592 | tf_op jit(solution)/shard_map/reshape | solution.py:60
  126.4 5.1 %convolution_convert_fusion = bf16[768,2,1536]{2,0,1:T(8,128)(2,1)} fusion(bf16[1,256,1536]{2,1,0:T(8,128)(2,1)} %copy-done.21, bf16[1,256,1536]{2,1,0:T(8,128)(2,1)} %copy-done.20, f32[1,256,768]{2,1,0:T(8,128)S(1)} %get-tuple-element.74, f32[768]{0:T(1024)} %get-tuple-element.65, f32[768]{0:T(1024)S(1)} %get-tuple-element.66, f32[256]{0:T(256)} %copy-done.44, ...), kind=kOutput, calls=%fused_computation.19 | convolution fusion | flops 1214447616 | bytes 7086080 | tf_op jit(solution)/shard_map/cld,tclf->dtf/dot_general | solution.py:145
  131.6 9.3 %copy.107 = bf16[768,2,1536]{2,1,0:T(2,128)(2,1)} copy(bf16[768,2,1536]{2,0,1:T(8,128)(2,1)} %convolution_convert_fusion) | data formatting | bytes 9437184 | tf_op jit(solution)/shard_map/convert.10
  140.9 11.4 %reshape.1011 = bf16[16,1152,128]{2,1,0:T(8,128)(2,1)} reshape(bf16[768,2,1536]{2,1,0:T(2,128)(2,1)} %copy.107) | data formatting | bytes 9437184 | tf_op jit(solution)/shard_map/reshape | solution.py:60
  152.3 2.5 multiply_reduce_fusion.2
  158.0 2.5 convolution_convert_fusion.6
  170.8 2.9 copy.105
  173.7 5.4 %reshape.1009 = bf16[16,432,128]{2,1,0:T(8,128)(2,1)} reshape(bf16[768,3,384]{2,1,0:T(4,128)(2,1)} %copy.105) | data formatting | bytes 3538944 | tf_op jit(solution)/shard_map/reshape | solution.py:60
  179.0 7.3 %pad_maximum_fusion = bf16[16,2304,128]{2,1,0:T(8,128)(2,1)} fusion(bf16[16,576,128]{2,1,0:T(8,128)(2,1)} %reshape.1012, bf16[16,1152,128]{2,1,0:T(8,128)(2,1)} %reshape.1011, bf16[16,144,128]{2,1,0:T(8,128)(2,1)S(1)} %reshape.1010, bf16[16,432,128]{2,1,0:T(8,128)(2,1)} %reshape.1009), kind=kLoop, calls=%fused_computation.18 | loop fusion | flops 37748736 | bytes 18874368 | tf_op jit(solution)/shard_map/concatenate | solution.py:182
  189.9 3.5 %all-to-all-start.1 = ((bf16[2,1,6,128,256]{3,4,2,1,0:T(8,128)(2,1)}), bf16[2,1,6,128,256]{3,4,2,1,0:T(8,128)(2,1)S(1)}, u32[]{:S(2)}, u32[]{:S(2)}) async-start(bf16[2,1,6,128,256]{3,4,2,1,0:T(8,128)(2,1)} %pad_maximum_fusion.4), calls=%async_computation.1 | async-start | bytes 1572864 | tf_op jit(solution)/shard_map/all_to_all | solution.py:205
  194.2 2.8 fusion.47
  199.1 6.4 %all-to-all-done.1 = bf16[2,1,6,128,256]{3,4,2,1,0:T(8,128)(2,1)S(1)} async-done(((bf16[2,1,6,128,256]{3,4,2,1,0:T(8,128)(2,1)}), bf16[2,1,6,128,256]{3,4,2,1,0:T(8,128)(2,1)S(1)}, u32[]{:S(2)}, u32[]{:S(2)}) %all-to-all-start.1) | async-done | bytes 786464 | tf_op jit(solution)/shard_map/all_to_all | solution.py:205
  207.4 9.7 %fusion.51 = f32[256,12]{1,0:T(8,128)S(1)} fusion(bf16[12,128,256]{2,0,1:T(8,128)(2,1)} %copy.100, bf16[1,128,256,256]{2,3,1,0:T(8,128)(2,1)} %copy.85, f32[256]{0:T(256)S(1)} %copy-done.52, f32[128,256]{1,0:T(8,128)S(1)} %copy-done.29, f32[128,256]{1,0:T(8,128)S(1)} %copy-done.19), kind=kOutput, calls=%fused_computation.73 | convolution fusion | flops 243269632 | bytes 17839104 | tf_op jit(solution)/shard_map/cqkp,chqk->ph/dot_general | solution.py:208
  218.9 21.7 %fusion.12 = (f32[256]{0:T(256)S(1)}, f32[128,256]{1,0:T(8,128)S(1)}, f32[128,256,256]{1,2,0:T(8,128)}) fusion(bf16[1,128,256,256]{2,3,1,0:T(8,128)(2,1)} %copy.85, f32[128,256]{1,0:T(8,128)S(1)} %copy-done.29, f32[128,256]{1,0:T(8,128)S(1)} %copy-done.19, f32[256]{0:T(256)S(1)} %copy-done.53, bf16[12,128,256]{2,0,1:T(8,128)(2,1)} %copy.100, ...), kind=kOutput, calls=%fused_computation.14 | convolution fusion | flops 268402432 | bytes 51519488 | tf_op jit(solution)/shard_map/chqk,ph->cqkp/dot_general | solution.py:211
  241.2 14.8 %multiply_reduce_fusion = f32[128,256]{1,0:T(8,128)S(1)} fusion(f32[128,256,256]{1,2,0:T(8,128)} %get-tuple-element.104, f32[256]{0:T(256)S(1)} %copy-done.53), kind=kLoop, calls=%fused_computation.16 | loop fusion | flops 16744448 | bytes 33686528 | tf_op jit(solution)/shard_map/reduce_sum | solution.py:20
  257.0 2.5 convolution_multiply_fusion.2
  259.5 25.2 %fusion.11 = bf16[1,128,256,256]{2,3,1,0:T(8,128)(2,1)} fusion(bf16[1,128,256,256]{2,3,1,0:T(8,128)(2,1)} %copy.85, f32[128,256,256]{1,2,0:T(8,128)} %get-tuple-element.104, f32[128,256]{1,0:T(8,128)S(1)} %broadcast_multiply_fusion, f32[128,256]{1,0:T(8,128)S(1)} %broadcast_multiply_fusion.1, f32[256]{0:T(256)S(1)} %copy-done.53, ...), kind=kLoop, calls=%fused_computation.13 | loop fusion | flops 75497472 | bytes 67634176 | tf_op jit(solution)/shard_map/convert_element_type | solution.py:215
  284.7 22.4 %copy.108 = bf16[1,128,256,256]{3,2,1,0:T(8,128)(2,1)} copy(bf16[1,128,256,256]{2,3,1,0:T(8,128)(2,1)} %fusion.11) | data formatting | bytes 33554432
  307.2 23.3 %all-gather = f32[16,1,8960]{2,1,0:T(1,128)S(1)} all-gather(f32[1,1,8960]{2,1,0:T(1,128)S(1)} %bitcast.231), channel_id=1, replica_groups=mesh['dp'=16,'head'=2] {'dp'}, dimensions={0}, use_global_device_ids=true | all-gather | bytes 609280 | tf_op jit(solution)/shard_map/all_gather | solution.py:218
  333.2 4.2 %fusion.74 = f32[256,4608]{1,0:T(8,128)} fusion(bf16[16,256]{1,0:T(8,128)(2,1)S(1)} %multiply_convert_fusion.8, f32[16,8960]{1,0:T(8,128)S(1)} %bitcast.205), kind=kOutput, calls=%fused_computation.129 | convolution fusion | flops 226492416 | bytes 5021696 | tf_op jit(solution)/shard_map/dot_general | solution.py:232
  (231 shorter events, 67.3 us)
Async XLA Ops:
  7.2 107.0 %copy-start = (bf16[1536,768]{1,0:T(8,128)(2,1)S(1)}, bf16[1536,768]{1,0:T(8,128)(2,1)}, u32[]{:S(2)}) copy-start(bf16[1536,768]{1,0:T(8,128)(2,1)} %param.28) | copy-start | bytes 7077892
  7.2 56.3 %collective-permute-start = (bf16[1,128,768]{2,1,0:T(8,128)(2,1)}, bf16[1,128,768]{2,1,0:T(8,128)(2,1)S(1)}, u32[]{:S(2)}, u32[]{:S(2)}) collective-permute-start(bf16[1,128,768]{2,1,0:T(8,128)(2,1)} %param.15), channel_id=1, source_target_pairs={{0,1},{1,0},{2,3},{3,2},{4,5},{5,4},{6,7},{7,6},{8,9},{9,8},{10,11... | collective-permute-start | bytes 589832 | tf_op jit(solution)/shard_map/ppermute | solution.py:35
  32.6 10.7 %copy-start.2 = (bf16[1,128,256,256]{2,3,1,0:T(8,128)(2,1)S(1)}, bf16[1,128,256,256]{2,3,1,0:T(8,128)(2,1)}, u32[]{:S(2)}) copy-start(bf16[1,128,256,256]{2,3,1,0:T(8,128)(2,1)} %copy.85) | copy-start | bytes 50331652
  53.2 6.1 %copy-start.47 = (f32[1,256]{1,0:T(1,128)S(1)}, f32[1,256]{1,0:T(1,128)}, u32[]{:S(2)}) copy-start(f32[1,256]{1,0:T(1,128)} %param.17) | copy-start | bytes 3076
  54.4 7.7 %copy-start.57 = (s32[1,256]{1,0:T(1,128)S(1)}, s32[1,256]{1,0:T(1,128)}, u32[]{:S(2)}) copy-start(s32[1,256]{1,0:T(1,128)} %param.19) | copy-start | bytes 3076
  54.4 9.1 %copy-start.8 = (bf16[1,128,768]{2,1,0:T(8,128)(2,1)S(1)}, bf16[1,128,768]{2,1,0:T(8,128)(2,1)}, u32[]{:S(2)}) copy-start(bf16[1,128,768]{2,1,0:T(8,128)(2,1)} %param.15) | copy-start | bytes 589828
  54.4 17.9 %all-to-all-start = ((bf16[1,12,128,256]{3,2,0,1:T(8,128)(2,1)}), bf16[1,12,128,256]{3,2,0,1:T(8,128)(2,1)S(1)}, u32[]{:S(2)}, u32[]{:S(2)}) async-start(bf16[1,12,128,256]{3,2,0,1:T(8,128)(2,1)} %copy.87), calls=%async_computation | async-start | bytes 1572864 | tf_op jit(solution)/shard_map/all_to_all | solution.py:103
  58.0 279.4 %reduce-scatter.2.cloned.1.call-start = ((), (), s32[]{:S(2)}) async-start(), calls=%async_computation.3 | async-start | bytes 10027008 | tf_op jit(solution)/shard_map/reduce_scatter | solution.py:191
  85.7 23.4 %copy-start.39 = (f32[768]{0:T(1024)S(1)}, f32[768]{0:T(1024)}, u32[]{:S(2)}) copy-start(f32[768]{0:T(1024)} %param.26) | copy-start | bytes 9220
  88.3 22.1 %copy-start.38 = (f32[768]{0:T(1024)S(1)}, f32[768]{0:T(1024)}, u32[]{:S(2)}) copy-start(f32[768]{0:T(1024)} %get-tuple-element.65) | copy-start | bytes 9220
  88.7 20.5 %copy-start.4 = (f32[1,256,768]{2,1,0:T(8,128)}, f32[1,256,768]{2,1,0:T(8,128)S(1)}, u32[]{:S(2)}) copy-start(f32[1,256,768]{2,1,0:T(8,128)S(1)} %convolution_bitcast_fusion) | copy-start | bytes 2359300
  88.7 20.5 %collective-permute-start.1 = (f32[1,256,768]{2,1,0:T(8,128)S(1)}, f32[1,256,768]{2,1,0:T(8,128)S(1)}, u32[]{:S(2)}, u32[]{:S(2)}) collective-permute-start(f32[1,256,768]{2,1,0:T(8,128)S(1)} %convolution_bitcast_fusion), channel_id=1, source_target_pairs={{0,1},{1,0},{2,3},{3,2},{4,5},{5,4},{6,7},{7,6},{8,9},{9,8},{10,11... | collective-permute-start | bytes 2359304 | tf_op jit(solution)/shard_map/ppermute | solution.py:35
  90.7 27.2 %collective-permute-start.3 = (bf16[1,128,768]{2,1,0:T(8,128)(2,1)}, bf16[1,128,768]{2,1,0:T(8,128)(2,1)S(1)}, u32[]{:S(2)}, u32[]{:S(2)}) collective-permute-start(bf16[1,128,768]{2,1,0:T(8,128)(2,1)} %param.29), channel_id=1, source_target_pairs={{0,1},{1,0},{2,3},{3,2},{4,5},{5,4},{6,7},{7,6},{8,9},{9,8},{10,11... | collective-permute-start | bytes 589832 | tf_op jit(solution)/shard_map/ppermute | solution.py:35
  115.9 71.1 %collective-permute-start.2 = (bf16[1,256,768]{2,1,0:T(8,128)(2,1)}, bf16[1,256,768]{2,1,0:T(8,128)(2,1)}, u32[]{:S(2)}, u32[]{:S(2)}) collective-permute-start(bf16[1,256,768]{2,1,0:T(8,128)(2,1)} %fusion.48), channel_id=1, source_target_pairs={{0,1},{1,0},{2,3},{3,2},{4,5},{5,4},{6,7},{7,6},{8,9},{9,8},{10,11... | collective-permute-start | bytes 1179656 | tf_op jit(solution)/shard_map/ppermute | solution.py:35
  121.4 30.9 %collective-permute-start.4 = (f32[1,256,768]{2,1,0:T(8,128)}, f32[1,256,768]{2,1,0:T(8,128)}, u32[]{:S(2)}, u32[]{:S(2)}) collective-permute-start(f32[1,256,768]{2,1,0:T(8,128)} %fusion.42), channel_id=1, source_target_pairs={{0,1},{1,0},{2,3},{3,2},{4,5},{5,4},{6,7},{7,6},{8,9},{9,8},{10,11... | collective-permute-start | bytes 2359304 | tf_op jit(solution)/shard_map/ppermute | solution.py:35
  140.9 11.5 %copy-start.45 = (f32[256]{0:T(256)S(1)}, f32[256]{0:T(256)}, u32[]{:S(2)}) copy-start(f32[256]{0:T(256)} %copy-done.44) | copy-start | bytes 3076
  163.3 5.4 %copy-start.50 = (f32[256]{0:T(256)S(1)}, f32[256]{0:T(256)}, u32[]{:S(2)}) copy-start(f32[256]{0:T(256)} %copy-done.49) | copy-start | bytes 3076
  163.3 5.4 %copy-start.55 = (f32[256]{0:T(256)S(1)}, f32[256]{0:T(256)}, u32[]{:S(2)}) copy-start(f32[256]{0:T(256)} %copy-done.54) | copy-start | bytes 3076
  189.9 15.6 %all-to-all-start.1 = ((bf16[2,1,6,128,256]{3,4,2,1,0:T(8,128)(2,1)}), bf16[2,1,6,128,256]{3,4,2,1,0:T(8,128)(2,1)S(1)}, u32[]{:S(2)}, u32[]{:S(2)}) async-start(bf16[2,1,6,128,256]{3,4,2,1,0:T(8,128)(2,1)} %pad_maximum_fusion.4), calls=%async_computation.1 | async-start | bytes 1572864 | tf_op jit(solution)/shard_map/all_to_all | solution.py:205
  194.2 13.2 %copy-start.19 = (f32[128,256]{1,0:T(8,128)S(1)}, f32[128,256]{1,0:T(8,128)}, u32[]{:S(2)}) copy-start(f32[128,256]{1,0:T(8,128)} %copy-done.18) | copy-start | bytes 393220
  194.2 13.2 %copy-start.29 = (f32[128,256]{1,0:T(8,128)S(1)}, f32[128,256]{1,0:T(8,128)}, u32[]{:S(2)}) copy-start(f32[128,256]{1,0:T(8,128)} %copy-done.28) | copy-start | bytes 393220
  194.2 13.2 %copy-start.52 = (f32[256]{0:T(256)S(1)}, f32[256]{0:T(256)}, u32[]{:S(2)}) copy-start(f32[256]{0:T(256)} %param.23) | copy-start | bytes 3076
  197.0 20.2 %collective-permute-start.5 = (bf16[1,256,768]{2,1,0:T(8,128)(2,1)S(1)}, bf16[1,256,768]{2,1,0:T(8,128)(2,1)}, u32[]{:S(2)}, u32[]{:S(2)}) collective-permute-start(bf16[1,256,768]{2,1,0:T(8,128)(2,1)S(1)} %fusion.47), channel_id=1, source_target_pairs={{0,1},{1,0},{2,3},{3,2},{4,5},{5,4},{6,7},{7,6},{8,9},{9,8},{10,11... | collective-permute-start | bytes 1179656 | tf_op jit(solution)/shard_map/ppermute | solution.py:35
  218.9 22.2 %copy-start.42 = (f32[768]{0:T(1024)S(1)}, f32[768]{0:T(1024)}, u32[]{:S(2)}) copy-start(f32[768]{0:T(1024)} %get-tuple-element.58) | copy-start | bytes 9220
  218.9 22.2 %copy-start.35 = (f32[768]{0:T(1024)S(1)}, f32[768]{0:T(1024)}, u32[]{:S(2)}) copy-start(f32[768]{0:T(1024)} %get-tuple-element.54) | copy-start | bytes 9220
  218.9 22.2 %copy-start.34 = (f32[768]{0:T(1024)S(1)}, f32[768]{0:T(1024)}, u32[]{:S(2)}) copy-start(f32[768]{0:T(1024)} %get-tuple-element.59) | copy-start | bytes 9220
  240.6 66.5 %collective-permute-start.6 = (f32[1,3328]{1,0:T(1,128)S(1)}, f32[1,3328]{1,0:T(1,128)S(1)}, u32[]{:S(2)}, u32[]{:S(2)}) collective-permute-start(f32[1,3328]{1,0:T(1,128)S(1)} %broadcast_in_dim.17), channel_id=1, source_target_pairs={{0,1},{1,0},{2,3},{3,2},{4,5},{5,4},{6,7},{7,6},{8,9},{9,8},{10,11... | collective-permute-start | bytes 39944 | tf_op jit(solution)/shard_map/ppermute | solution.py:35
  241.2 14.9 %copy-start.58 = (f32[128]{0:T(128)S(1)}, f32[128]{0:T(128)}, u32[]{:S(2)}) copy-start(f32[128]{0:T(128)} %dynamic-slice.2) | copy-start | bytes 1540
  241.2 15.8 %copy-start.3 = (bf16[256,4608]{1,0:T(8,128)(2,1)S(1)}, bf16[256,4608]{1,0:T(8,128)(2,1)}, u32[]{:S(2)}) copy-start(bf16[256,4608]{1,0:T(8,128)(2,1)} %param.20) | copy-start | bytes 7077892
  241.2 15.8 %copy-start.48 = (f32[1,256]{1,0:T(1,128)S(1)}, f32[1,256]{1,0:T(1,128)}, u32[]{:S(2)}) copy-start(f32[1,256]{1,0:T(1,128)} %param.17) | copy-start | bytes 3076
  284.7 22.5 %copy-start.41 = (f32[768]{0:T(1024)S(1)}, f32[768]{0:T(1024)}, u32[]{:S(2)}) copy-start(f32[768]{0:T(1024)} %get-tuple-element.57) | copy-start | bytes 9220
  337.4 5.5 %copy-start.13 = (bf16[1,2304,128]{2,1,0:T(8,128)(2,1)S(1)}, bf16[1,2304,128]{2,1,0:T(8,128)(2,1)}, u32[]{:S(2)}) copy-start(bf16[1,2304,128]{2,1,0:T(8,128)(2,1)} %reduce-scatter.2.cloned.1.call-done) | copy-start | bytes 1769476
  (41 other events, 115.3 us)
Sparse Core Ops, SparseCore 0:
  186.5 112.8 reduce-scatter.1
